TPU v7x, 32 devices: a whole 2x2x4 slice. The times are simulated.
32 devices in a mesh: dp: 8 (over y, x, core), space: 4 (over z).
Axes of the slice: x: 2, y: 2, z: 4, core: 2. Of those that a mesh axis runs over, the one named last changes fastest.
Arguments:
- volume: bfloat16 [8, 32, 8, 16, 128], P('dp', None, 'space')
- out_grad: bfloat16 [8, 32, 8, 16, 128], P('dp', None, 'space'), may hold values from -0.016479492 to 0.016479492
- kernel: bfloat16 [32, 864], replicated, may hold values from -0.21875 to 0.21875
- sample_idx: int32 [8, 4096], P('dp', 'space'), may hold values from 0 to 4095
- a_inverse: float32 [864, 864], P('space')
- g_inverse: float32 [32, 32], replicated
Outputs:
- conv_out: bfloat16 [8, 32, 8, 16, 128], P('dp', None, 'space')
- a_factor: float32 [864, 864], P('dp', 'space')
- g_factor: float32 [32, 32], replicated
- pre_grad: float32 [32, 864], replicated
Inputs may be any that keep to these rules, and one draw needn't show every extreme that they name: `sample_idx`: column s of a sample's row names a cell of slab s // 1024, as the number z * 16 * 128 + y * 128 + x counted within that slab of 2 planes.
All inputs are finite; a program needn't handle non-finite values.
Results may differ from a plain program's by a relative error of at most 0.0085.
Values may be sent and summed in bfloat16 or wider, within the bound.
No kernel may reach another device: no remote copies, remote signals or barrier semaphores. Data moves between devices by JAX's collectives and lax.ppermute only.
A program may use at most 128 MiB of HBM per device.

v0:
```python
import jax
import jax.numpy as jnp
from jax import lax
from jax.sharding import PartitionSpec as P


def padded_2(cells, sides, width):
    for axis, dim in sides:
        count = lax.axis_size(axis)
        ends = count - 1
        head = lax.slice_in_dim(cells, 0, width, axis=dim)
        tail = lax.slice_in_dim(cells, cells.shape[dim] - width, cells.shape[dim], axis=dim)
        cells = jnp.concatenate(
            [
                lax.ppermute(tail, axis, [(i, (i + 1) % count) for i in range(ends)]),
                cells,
                lax.ppermute(head, axis, [((i + 1) % count, i) for i in range(ends)]),
            ],
            axis=dim,
        )
    return cells


def on_device(volume, out_grad, kernel, sample_idx, a_inverse, g_inverse):
    highest = lax.Precision.HIGHEST
    f32 = jnp.float32
    channels = volume.shape[1]
    planes = volume.shape[2]
    y_cells = volume.shape[3]
    x_cells = volume.shape[4]
    cells = planes * y_cells * x_cells
    patch = kernel.shape[1]
    n_dp = lax.axis_size("dp")
    n_sp = lax.axis_size("space")
    contract_cells = (((1,), (1,)), ((), ()))
    block = padded_2(volume, (("space", 2),), 1)
    padded = jnp.pad(block[0], ((0, 0), (0, 0), (1, 1), (1, 1)))
    taps = [
        padded[:, dz : dz + planes, dy : dy + y_cells, dx : dx + x_cells]
        for dz in range(3)
        for dy in range(3)
        for dx in range(3)
    ]
    patches_t = jnp.stack(taps, axis=1).reshape(patch, cells)
    grad_flat = out_grad[0].reshape(channels, cells)
    forward = jnp.dot(kernel, patches_t, preferred_element_type=f32)
    conv_out = forward.astype(jnp.bfloat16).reshape(1, channels, planes, y_cells, x_cells)
    grad_w = lax.dot_general(grad_flat, patches_t, contract_cells, preferred_element_type=f32)
    g_part = lax.dot_general(grad_flat, grad_flat, contract_cells, preferred_element_type=f32)
    cell_ids = sample_idx[0]
    counts = jnp.sum(
        (cell_ids[:, None] == jnp.arange(cells, dtype=jnp.int32)[None, :]).astype(f32), axis=0
    )
    weighted = patches_t.astype(f32) * counts[None, :]
    high = weighted.astype(jnp.bfloat16)
    low = (weighted - high.astype(f32)).astype(jnp.bfloat16)
    total_samples = sample_idx.shape[1] * n_sp * n_dp
    a_part = (
        lax.dot_general(high, patches_t, contract_cells, preferred_element_type=f32)
        + lax.dot_general(low, patches_t, contract_cells, preferred_element_type=f32)
    ) / jnp.float32(total_samples)
    rows = patch // n_dp
    cols = patch // n_sp
    a_blocks = (
        a_part.astype(jnp.bfloat16)
        .reshape(n_dp, rows, n_sp, cols)
        .transpose(0, 2, 1, 3)
        .reshape(n_dp * n_sp, rows, cols)
    )
    a_factor = lax.psum_scatter(a_blocks, ("dp", "space"), scatter_dimension=0, tiled=True)
    a_factor = a_factor.reshape(rows, cols).astype(f32)
    both = lax.psum(jnp.concatenate([grad_w, g_part], axis=1), ("dp", "space"))
    grad_sum = both[:, :patch]
    g_factor = both[:, patch:]
    left = jnp.dot(g_inverse, grad_sum, precision=highest)
    own_rows = a_inverse.shape[0]
    left_rows = lax.dynamic_slice_in_dim(left, lax.axis_index("space") * own_rows, own_rows, axis=1)
    pre_grad = lax.psum(jnp.dot(left_rows, a_inverse, precision=highest), "space")
    return (conv_out, a_factor, g_factor, pre_grad)


def solution(mesh):
    placed = (
        P("dp", None, "space", None, None),
        P("dp", None, "space", None, None),
        P(),
        P("dp", "space"),
        P("space", None),
        P(),
    )
    return jax.shard_map(
        on_device,
        mesh=mesh,
        in_specs=placed,
        out_specs=(P("dp", None, "space", None, None), P("dp", "space"), P(), P()),
        check_vma=False,
    )
```

profile of v0, /device:TPU:0, one launch (start us, length us, event | category | flops | bytes accessed | tf_op | source)
XLA Modules:
  0.0 373.9 jit_solution(7109457592317233880)
XLA Ops:
  7.2 1.1 fusion.59
  8.3 4.9 %collective-permute-start = (bf16[1,32,1,16,128]{4,3,2,1,0:T(8,128)(2,1)S(1)}, bf16[1,32,1,16,128]{4,3,2,1,0:T(8,128)(2,1)S(1)}, u32[]{:S(2)}, u32[]{:S(2)}) collective-permute-start(bf16[1,32,1,16,128]{4,3,2,1,0:T(8,128)(2,1)S(1)} %get-tuple-element.6), channel_id=1, source_target_pairs={{0,1},{1,2},{2,3},{4,5},{5,6},{6,7},{8,9},{9,10},{10,11},{12,13},{... | collective-permute-start | bytes 393224 | tf_op jit(solution)/shard_map/ppermute | solution.py:15
  13.2 1.3 collective-permute-start.1
  14.5 3.4 convert_reduce_fusion
  17.9 1.1 reshape_squeeze.3
  19.0 1.3 convolution_bitcast_fusion.1
  20.3 1.0 maximum_bitcast_fusion
  24.4 0.2 fusion.39
  25.6 4.6 %copy.25 = bf16[32,27,2,16,128]{4,3,2,1,0:T(8,128)(2,1)} copy(bf16[32,27,2,16,128]{4,3,2,0,1:T(8,128)(2,1)S(1)} %fusion.49) | data formatting | bytes 14155776 | tf_op jit(solution)/shard_map/stack | solution.py:44
  30.2 0.7 copy-done.1
  30.8 12.0 %subtract_convert_fusion = (bf16[32,27,2,16,128]{4,3,2,0,1:T(8,128)(2,1)}, bf16[32,27,2,16,128]{4,3,2,0,1:T(8,128)(2,1)}) fusion(bf16[32,27,2,16,128]{4,3,2,0,1:T(8,128)(2,1)} %copy-done.1, f32[2,16,128]{2,1,0:T(8,128)S(1)} %bitcast.151), kind=kLoop, calls=%fused_computation.2 | loop fusion | flops 21233664 | bytes 21250048 | tf_op jit(solution)/shard_map/convert_element_type | solution.py:56
  42.9 7.1 %copy.26 = bf16[32,27,2,16,128]{4,3,2,1,0:T(8,128)(2,1)} copy(bf16[32,27,2,16,128]{4,3,2,0,1:T(8,128)(2,1)} %get-tuple-element.5) | data formatting | bytes 14155776 | tf_op jit(solution)/shard_map/convert_element_type | solution.py:55
  50.0 11.6 %convert_element_type.83 = bf16[864,4096]{1,0:T(8,128)(2,1)} reshape(bf16[32,27,2,16,128]{4,3,2,1,0:T(8,128)(2,1)} %copy.26) | data formatting | bytes 14155776 | tf_op jit(solution)/shard_map/convert_element_type | solution.py:55
  61.6 11.6 %reshape.94 = bf16[864,4096]{1,0:T(8,128)(2,1)} reshape(bf16[32,27,2,16,128]{4,3,2,1,0:T(8,128)(2,1)} %copy.25) | data formatting | bytes 14155776 | tf_op jit(solution)/shard_map/reshape | solution.py:44
  73.2 7.1 %copy.27 = bf16[32,27,2,16,128]{4,3,2,1,0:T(8,128)(2,1)} copy(bf16[32,27,2,16,128]{4,3,2,0,1:T(8,128)(2,1)} %get-tuple-element.4) | data formatting | bytes 14155776 | tf_op jit(solution)/shard_map/convert_element_type | solution.py:56
  80.3 11.6 %convert_element_type.86 = bf16[864,4096]{1,0:T(8,128)(2,1)} reshape(bf16[32,27,2,16,128]{4,3,2,1,0:T(8,128)(2,1)} %copy.27) | data formatting | bytes 14155776 | tf_op jit(solution)/shard_map/convert_element_type | solution.py:56
  91.9 12.9 %fusion.60 = f32[864,864]{1,0:T(8,128)} fusion(bf16[864,4096]{1,0:T(8,128)(2,1)} %convert_element_type.83, bf16[864,4096]{1,0:T(8,128)(2,1)} %reshape.94), kind=kOutput, calls=%fused_computation.98 | convolution fusion | flops 6115295232 | bytes 17141760 | tf_op jit(solution)/shard_map/dot_general | solution.py:59
  104.8 5.1 %convolution_bitcast_fusion = f32[32,864]{1,0:T(8,128)S(1)} fusion(bf16[864,4096]{1,0:T(8,128)(2,1)} %reshape.94, bf16[32,4096]{1,0:T(8,128)(2,1)S(1)} %reshape_squeeze.3), kind=kOutput, calls=%fused_computation.32 | convolution fusion | flops 226492416 | bytes 7450624 | tf_op jit(solution)/shard_map/dot_general | solution.py:48
  109.9 0.7 pad_maximum_fusion
  110.7 13.3 %multiply_convert_fusion = bf16[864,864]{1,0:T(8,128)(2,1)} fusion(f32[864,864]{1,0:T(8,128)} %fusion.60, bf16[864,4096]{1,0:T(8,128)(2,1)} %convert_element_type.86, bf16[864,4096]{1,0:T(8,128)(2,1)} %reshape.94), kind=kOutput, calls=%fused_computation.30 | convolution fusion | flops 6117534720 | bytes 18634752 | tf_op jit(solution)/shard_map/dot_general | solution.py:60
  124.0 4.6 %reshape.96 = bf16[8,108,4,216]{3,2,1,0:T(4,128)(2,1)S(1)} reshape(bf16[864,864]{1,0:T(8,128)(2,1)} %multiply_convert_fusion) | data formatting | bytes 2985984 | tf_op jit(solution)/shard_map/reshape | solution.py:66
  128.6 2.6 copy.28
  131.2 4.4 %fusion.1 = bf16[4,8,32,128]{3,1,2,0:T(8,128)(2,1)S(1)} fusion(bf16[32,864]{1,0:T(8,128)(2,1)S(1)} %copy-done.2, bf16[864,4096]{1,0:T(8,128)(2,1)} %reshape.94), kind=kOutput, calls=%fused_computation.31 | convolution fusion | flops 226623488 | bytes 7395328 | tf_op jit(solution)/shard_map/dot_general | solution.py:46
  135.6 0.8 copy.32
  136.3 97.5 %all-reduce.5.cloned.1.call-done = f32[32,896]{1,0:T(8,128)} async-done(((f32[32,896]{1,0:T(8,128)}), f32[32,896]{1,0:T(8,128)}) %all-reduce.5.cloned.1.call-update) | async-done | bytes 114704 | tf_op jit(solution)/shard_map/psum | solution.py:72
  233.8 1.1 fusion.54
  235.0 1.3 fusion.56
  236.3 1.4 slice.130
  237.7 92.0 %reduce-scatter.4.cloned.1.call-done = bf16[1,108,216]{1,2,0:T(8,128)(2,1)} async-done(((bf16[32,108,216]{1,2,0:T(8,128)(2,1)}), bf16[1,108,216]{1,2,0:T(8,128)(2,1)}) %reduce-scatter.4.cloned.1.call-update) | async-done | bytes 46672
  329.7 1.5 bitcast_convert_fusion
  331.2 34.7 %all-reduce.7.cloned.1.call-done = f32[32,864]{1,0:T(8,128)} async-done(((f32[32,864]{1,0:T(8,128)}), f32[32,864]{1,0:T(8,128)}) %all-reduce.7.cloned.1.call-update) | async-done | bytes 110608 | tf_op jit(solution)/shard_map/psum | solution.py:78
  365.9 1.6 copy.63
  (41 shorter events, 4.1 us)
Async XLA Ops:
  7.2 227.8 %copy-start = (f32[216,864]{1,0:T(8,128)S(1)}, f32[216,864]{1,0:T(8,128)}, u32[]{:S(2)}) copy-start(f32[216,864]{1,0:T(8,128)} %param.10) | copy-start | bytes 2239492
  7.2 226.7 %all-reduce.5.cloned.1.call-start = ((), (), s32[]{:S(2)}) async-start(), calls=%async_computation.1 | async-start | bytes 229376 | tf_op jit(solution)/shard_map/psum | solution.py:72
  8.3 12.0 %collective-permute-start = (bf16[1,32,1,16,128]{4,3,2,1,0:T(8,128)(2,1)S(1)}, bf16[1,32,1,16,128]{4,3,2,1,0:T(8,128)(2,1)S(1)}, u32[]{:S(2)}, u32[]{:S(2)}) collective-permute-start(bf16[1,32,1,16,128]{4,3,2,1,0:T(8,128)(2,1)S(1)} %get-tuple-element.6), channel_id=1, source_target_pairs={{0,1},{1,2},{2,3},{4,5},{5,6},{6,7},{8,9},{9,10},{10,11},{12,13},{... | collective-permute-start | bytes 393224 | tf_op jit(solution)/shard_map/ppermute | solution.py:15
  13.2 7.0 %collective-permute-start.1 = (bf16[1,32,1,16,128]{4,3,2,1,0:T(8,128)(2,1)S(1)}, bf16[1,32,1,16,128]{4,3,2,1,0:T(8,128)(2,1)S(1)}, u32[]{:S(2)}, u32[]{:S(2)}) collective-permute-start(bf16[1,32,1,16,128]{4,3,2,1,0:T(8,128)(2,1)S(1)} %get-tuple-element.7), channel_id=1, source_target_pairs={{1,0},{2,1},{3,2},{5,4},{6,5},{7,6},{9,8},{10,9},{11,10},{13,12},{... | collective-permute-start | bytes 393224 | tf_op jit(solution)/shard_map/ppermute | solution.py:17
  25.6 5.3 %copy-start.1 = (bf16[32,27,2,16,128]{4,3,2,0,1:T(8,128)(2,1)}, bf16[32,27,2,16,128]{4,3,2,0,1:T(8,128)(2,1)S(1)}, u32[]{:S(2)}) copy-start(bf16[32,27,2,16,128]{4,3,2,0,1:T(8,128)(2,1)S(1)} %fusion.49) | copy-start | bytes 21233668
  110.7 219.0 %reduce-scatter.4.cloned.1.call-start = ((), (), s32[]{:S(2)}) async-start(), calls=%async_computation.3 | async-start | bytes 1824768
  124.0 7.2 %copy-start.2 = (bf16[32,864]{1,0:T(8,128)(2,1)S(1)}, bf16[32,864]{1,0:T(8,128)(2,1)}, u32[]{:S(2)}) copy-start(bf16[32,864]{1,0:T(8,128)(2,1)} %param.8) | copy-start | bytes 165892
  128.5 105.3 %copy-start.3 = (f32[32,32]{1,0:T(8,128)S(1)}, f32[32,32]{1,0:T(8,128)}, u32[]{:S(2)}) copy-start(f32[32,32]{1,0:T(8,128)} %param.11) | copy-start | bytes 12292
  131.1 234.7 %all-reduce.7.cloned.1.call-start = ((), (), s32[]{:S(2)}) async-start(), calls=%async_computation.2 | async-start | bytes 229376 | tf_op jit(solution)/shard_map/psum | solution.py:78
Sparse Core Ops, SparseCore 0:
  110.8 123.0 all-reduce.4
  239.2 90.4 reduce-scatter.3
  332.7 33.1 all-reduce.6
where the time goes:
time: 375 us; the launch traced here: 374 us
  waiting for transfers between devices  224 us (60%)
  local copies, waits for them, and re-layouts  71.4 us (19%)
  matrix products  39.4 us (11%)
  other arithmetic  18.6 us (5%)
  between operations  14 us (4%)
  starting transfers between devices  6.35 us (2%)
    psum x1, waiting for transfers between devices, on_device(): both = lax.psum(jnp.concatenate([grad_w, g_part], axis=1), ('dp', 'space'))  97.5 us
    unnamed x4, waiting for transfers between devices  92 us
    psum x1, waiting for transfers between devices, on_device(): lax.psum(jnp.dot(left_rows, a_inverse, precision=highest), 'space')  34.7 us
    convert_element_type x2, local copies, waits for them, and re-layouts, on_device(): high = weighted.astype(jnp.bfloat16)  18.8 us
    convert_element_type x2, local copies, waits for them, and re-layouts, on_device(): low = (weighted - high.astype(f32)).astype(jnp.bfloat16)  18.6 us
    dot_general x1, matrix products, on_device(): lax.dot_general(low, patches_t, contract_cells, preferred_element_type=f32)  13.3 us
    dot_general x1, matrix products, on_device(): lax.dot_general(high, patches_t, contract_cells, preferred_element_type=f32)  12.9 us
    convert_element_type x1, other arithmetic, on_device(): low = (weighted - high.astype(f32)).astype(jnp.bfloat16)  12 us
  transfers between devices with their start and end apart: 5, of which 3 were waited for; matrix products, arithmetic and copies ran while one was open for 10% of the time, Pallas kernels for 0%

commit v1 on v0

--- a/solution.py
+++ b/solution.py
@@ -69,7 +69,8 @@
     )
     a_factor = lax.psum_scatter(a_blocks, ("dp", "space"), scatter_dimension=0, tiled=True)
     a_factor = a_factor.reshape(rows, cols).astype(f32)
-    both = lax.psum(jnp.concatenate([grad_w, g_part], axis=1), ("dp", "space"))
+    local_array = jnp.concatenate([grad_w, g_part], axis=1)
+    both = jnp.sum(lax.all_gather(local_array, ("dp", "space")), 0)
     grad_sum = both[:, :patch]
     g_factor = both[:, patch:]
     left = jnp.dot(g_inverse, grad_sum, precision=highest)

time: 375 us -> 267 us (0.71)
  waiting for transfers between devices: 224 us -> 118 us
  matrix products: 39.4 us -> 34.1 us
    psum x1 -> x0, waiting for transfers between devices: 97.5 us -> none  [on_device(): both = lax.psum(jnp.concatenate([grad_w, g_part], axis=1), ('dp', 'space'))]
    unnamed x4, waiting for transfers between devices: 92 us -> 81.3 us
    unnamed x36 -> x40, local copies, waits for them, and re-layouts: 6.94 us -> 9.2 us
  transfers between devices with their start and end apart: 5 -> 5, of which waited for: 3 -> 3; matrix products, arithmetic and copies ran while one was open for 10% -> 36% of each run, Pallas kernels for 0% -> 0%
where the time goes in v1:
time: 267 us; the launch traced here: 266 us
  waiting for transfers between devices  118 us (44%)
  local copies, waits for them, and re-layouts  72.4 us (27%)
  matrix products  34.1 us (13%)
  other arithmetic  20.3 us (8%)
  between operations  14 us (5%)
  starting transfers between devices  6.53 us (2%)
    unnamed x4, waiting for transfers between devices  81.3 us
    psum x1, waiting for transfers between devices, on_device(): lax.psum(jnp.dot(left_rows, a_inverse, precision=highest), 'space')  34 us
    convert_element_type x2, local copies, waits for them, and re-layouts, on_device(): low = (weighted - high.astype(f32)).astype(jnp.bfloat16)  18.8 us
    convert_element_type x2, local copies, waits for them, and re-layouts, on_device(): high = weighted.astype(jnp.bfloat16)  18.7 us
    convert_element_type x1, other arithmetic, on_device(): low = (weighted - high.astype(f32)).astype(jnp.bfloat16)  12 us
    reshape x1, local copies, waits for them, and re-layouts, on_device(): patches_t = jnp.stack(taps, axis=1).reshape(patch, cells)  11.6 us
    dot_general x1, matrix products, on_device(): lax.dot_general(high, patches_t, contract_cells, preferred_element_type=f32)  11 us
    dot_general x1, matrix products, on_device(): lax.dot_general(low, patches_t, contract_cells, preferred_element_type=f32)  10.8 us
  transfers between devices with their start and end apart: 5, of which 3 were waited for; matrix products, arithmetic and copies ran while one was open for 36% of the time, Pallas kernels for 0%

profile of v1, /device:TPU:0, one launch (start us, length us, event | category | flops | bytes accessed | tf_op | source)
XLA Modules:
  0.0 265.8 jit_solution(1556473297271966058)
XLA Ops:
  7.2 1.1 fusion.59
  8.3 4.9 %collective-permute-start = (bf16[1,32,1,16,128]{4,3,2,1,0:T(8,128)(2,1)S(1)}, bf16[1,32,1,16,128]{4,3,2,1,0:T(8,128)(2,1)S(1)}, u32[]{:S(2)}, u32[]{:S(2)}) collective-permute-start(bf16[1,32,1,16,128]{4,3,2,1,0:T(8,128)(2,1)S(1)} %get-tuple-element.6), channel_id=1, source_target_pairs={{0,1},{1,2},{2,3},{4,5},{5,6},{6,7},{8,9},{9,10},{10,11},{12,13},{... | collective-permute-start | bytes 393224 | tf_op jit(solution)/shard_map/ppermute | solution.py:15
  13.2 1.3 collective-permute-start.1
  14.5 1.1 reshape_squeeze.3
  15.6 1.3 convolution_bitcast_fusion.1
  16.9 3.2 %collective-permute-done.1 = bf16[1,32,1,16,128]{4,3,2,1,0:T(8,128)(2,1)S(1)} collective-permute-done((bf16[1,32,1,16,128]{4,3,2,1,0:T(8,128)(2,1)S(1)}, bf16[1,32,1,16,128]{4,3,2,1,0:T(8,128)(2,1)S(1)}, u32[]{:S(2)}, u32[]{:S(2)}) %collective-permute-start.1) | collective-permute-done | bytes 131104 | tf_op jit(solution)/shard_map/ppermute | solution.py:17
  20.1 1.0 maximum_bitcast_fusion
  25.4 2.9 %copy-done.1 = bf16[32,27,2,16,128]{4,3,2,0,1:T(8,128)(2,1)} copy-done((bf16[32,27,2,16,128]{4,3,2,0,1:T(8,128)(2,1)}, bf16[32,27,2,16,128]{4,3,2,0,1:T(8,128)(2,1)S(1)}, u32[]{:S(2)}) %copy-start.1) | copy-done | bytes 7077912
  28.3 4.0 %copy.25 = bf16[32,27,2,16,128]{4,3,2,1,0:T(8,128)(2,1)} copy(bf16[32,27,2,16,128]{4,3,2,0,1:T(8,128)(2,1)S(1)} %fusion.49) | data formatting | bytes 14155776 | tf_op jit(solution)/shard_map/stack | solution.py:44
  32.3 11.6 %reshape.94 = bf16[864,4096]{1,0:T(8,128)(2,1)} reshape(bf16[32,27,2,16,128]{4,3,2,1,0:T(8,128)(2,1)} %copy.25) | data formatting | bytes 14155776 | tf_op jit(solution)/shard_map/reshape | solution.py:44
  43.9 5.1 %convolution_bitcast_fusion = f32[32,864]{1,0:T(8,128)S(1)} fusion(bf16[864,4096]{1,0:T(8,128)(2,1)} %reshape.94, bf16[32,4096]{1,0:T(8,128)(2,1)S(1)} %reshape_squeeze.3), kind=kOutput, calls=%fused_computation.32 | convolution fusion | flops 226492416 | bytes 7450624 | tf_op jit(solution)/shard_map/dot_general | solution.py:48
  49.1 0.7 pad_maximum_fusion
  50.1 2.8 %convert_reduce_fusion = f32[4096]{0:T(1024)S(1)} fusion(s32[1024]{0:T(1024)S(1)} %bitcast.154), kind=kLoop, calls=%fused_computation | loop fusion | flops 12578816 | bytes 20480 | tf_op jit(solution)/shard_map/reduce_sum | solution.py:51
  52.8 12.0 %subtract_convert_fusion = (bf16[32,27,2,16,128]{4,3,2,0,1:T(8,128)(2,1)}, bf16[32,27,2,16,128]{4,3,2,0,1:T(8,128)(2,1)}) fusion(bf16[32,27,2,16,128]{4,3,2,0,1:T(8,128)(2,1)} %copy-done.1, f32[2,16,128]{2,1,0:T(8,128)S(1)} %bitcast.153), kind=kLoop, calls=%fused_computation.2 | loop fusion | flops 21233664 | bytes 21250048 | tf_op jit(solution)/shard_map/convert_element_type | solution.py:56
  64.9 7.1 %copy.26 = bf16[32,27,2,16,128]{4,3,2,1,0:T(8,128)(2,1)} copy(bf16[32,27,2,16,128]{4,3,2,0,1:T(8,128)(2,1)} %get-tuple-element.5) | data formatting | bytes 14155776 | tf_op jit(solution)/shard_map/convert_element_type | solution.py:55
  71.9 11.6 %convert_element_type.83 = bf16[864,4096]{1,0:T(8,128)(2,1)} reshape(bf16[32,27,2,16,128]{4,3,2,1,0:T(8,128)(2,1)} %copy.26) | data formatting | bytes 14155776 | tf_op jit(solution)/shard_map/convert_element_type | solution.py:55
  83.5 7.2 %copy.27 = bf16[32,27,2,16,128]{4,3,2,1,0:T(8,128)(2,1)} copy(bf16[32,27,2,16,128]{4,3,2,0,1:T(8,128)(2,1)} %get-tuple-element.4) | data formatting | bytes 14155776 | tf_op jit(solution)/shard_map/convert_element_type | solution.py:56
  90.7 11.6 %convert_element_type.86 = bf16[864,4096]{1,0:T(8,128)(2,1)} reshape(bf16[32,27,2,16,128]{4,3,2,1,0:T(8,128)(2,1)} %copy.27) | data formatting | bytes 14155776 | tf_op jit(solution)/shard_map/convert_element_type | solution.py:56
  102.3 11.0 %fusion.60 = f32[864,864]{1,0:T(8,128)S(1)} fusion(bf16[864,4096]{1,0:T(8,128)(2,1)} %convert_element_type.83, bf16[864,4096]{1,0:T(8,128)(2,1)} %reshape.94), kind=kOutput, calls=%fused_computation.98 | convolution fusion | flops 6115295232 | bytes 17141760 | tf_op jit(solution)/shard_map/dot_general | solution.py:59
  113.4 10.8 %multiply_convert_fusion = bf16[864,864]{1,0:T(8,128)(2,1)} fusion(f32[864,864]{1,0:T(8,128)S(1)} %fusion.60, bf16[864,4096]{1,0:T(8,128)(2,1)S(1)} %copy-done.2, bf16[864,4096]{1,0:T(8,128)(2,1)} %reshape.94), kind=kOutput, calls=%fused_computation.30 | convolution fusion | flops 6117534720 | bytes 18634752 | tf_op jit(solution)/shard_map/dot_general | solution.py:60
  124.2 4.6 %reshape.96 = bf16[8,108,4,216]{3,2,1,0:T(4,128)(2,1)S(1)} reshape(bf16[864,864]{1,0:T(8,128)(2,1)} %multiply_convert_fusion) | data formatting | bytes 2985984 | tf_op jit(solution)/shard_map/reshape | solution.py:66
  128.8 2.5 copy.28
  131.4 4.3 %fusion.1 = bf16[4,8,32,128]{3,1,2,0:T(8,128)(2,1)S(1)} fusion(bf16[32,864]{1,0:T(8,128)(2,1)S(1)} %copy-done.3, bf16[864,4096]{1,0:T(8,128)(2,1)} %reshape.94), kind=kOutput, calls=%fused_computation.31 | convolution fusion | flops 226623488 | bytes 7395328 | tf_op jit(solution)/shard_map/dot_general | solution.py:46
  135.7 0.8 copy.32
  136.5 2.2 reduce_sum.19
  138.8 0.2 fusion.54
  139.0 1.3 fusion.56
  140.3 81.2 %reduce-scatter.4.cloned.1.call-done = bf16[1,108,216]{1,2,0:T(8,128)(2,1)} async-done(((bf16[32,108,216]{1,2,0:T(8,128)(2,1)}), bf16[1,108,216]{1,2,0:T(8,128)(2,1)}) %reduce-scatter.4.cloned.1.call-update) | async-done | bytes 46672
  221.5 1.5 bitcast_convert_fusion
  223.0 0.7 slice.130
  223.7 34.0 %all-reduce.4.cloned.1.call-done = f32[32,864]{1,0:T(8,128)} async-done(((f32[32,864]{1,0:T(8,128)}), f32[32,864]{1,0:T(8,128)}) %all-reduce.4.cloned.1.call-update) | async-done | bytes 110608 | tf_op jit(solution)/shard_map/psum | solution.py:79
  257.7 1.6 copy.62
  (46 shorter events, 4.5 us)
Async XLA Ops:
  7.2 131.8 %copy-start = (f32[216,864]{1,0:T(8,128)S(1)}, f32[216,864]{1,0:T(8,128)}, u32[]{:S(2)}) copy-start(f32[216,864]{1,0:T(8,128)} %param.10) | copy-start | bytes 2239492
  7.2 129.3 %all-gather.3.cloned.1.call-start = ((), (), s32[]{:S(2)}) async-start(), calls=%async_computation.2 | async-start | bytes 3784704 | tf_op jit(solution)/shard_map/all_gather | solution.py:73
  8.3 8.6 %collective-permute-start = (bf16[1,32,1,16,128]{4,3,2,1,0:T(8,128)(2,1)S(1)}, bf16[1,32,1,16,128]{4,3,2,1,0:T(8,128)(2,1)S(1)}, u32[]{:S(2)}, u32[]{:S(2)}) collective-permute-start(bf16[1,32,1,16,128]{4,3,2,1,0:T(8,128)(2,1)S(1)} %get-tuple-element.6), channel_id=1, source_target_pairs={{0,1},{1,2},{2,3},{4,5},{5,6},{6,7},{8,9},{9,10},{10,11},{12,13},{... | collective-permute-start | bytes 393224 | tf_op jit(solution)/shard_map/ppermute | solution.py:15
  13.2 6.9 %collective-permute-start.1 = (bf16[1,32,1,16,128]{4,3,2,1,0:T(8,128)(2,1)S(1)}, bf16[1,32,1,16,128]{4,3,2,1,0:T(8,128)(2,1)S(1)}, u32[]{:S(2)}, u32[]{:S(2)}) collective-permute-start(bf16[1,32,1,16,128]{4,3,2,1,0:T(8,128)(2,1)S(1)} %get-tuple-element.7), channel_id=1, source_target_pairs={{1,0},{2,1},{3,2},{5,4},{6,5},{7,6},{9,8},{10,9},{11,10},{13,12},{... | collective-permute-start | bytes 393224 | tf_op jit(solution)/shard_map/ppermute | solution.py:17
  25.4 2.9 %copy-start.1 = (bf16[32,27,2,16,128]{4,3,2,0,1:T(8,128)(2,1)}, bf16[32,27,2,16,128]{4,3,2,0,1:T(8,128)(2,1)S(1)}, u32[]{:S(2)}) copy-start(bf16[32,27,2,16,128]{4,3,2,0,1:T(8,128)(2,1)S(1)} %fusion.49) | copy-start | bytes 21233668
  43.9 6.1 %copy-start.5 = (s32[1,1024]{1,0:T(1,128)S(1)}, s32[1,1024]{1,0:T(1,128)}, u32[]{:S(2)}) copy-start(s32[1,1024]{1,0:T(1,128)} %param.9) | copy-start | bytes 12292
  49.8 171.7 %reduce-scatter.4.cloned.1.call-start = ((), (), s32[]{:S(2)}) async-start(), calls=%async_computation.3 | async-start | bytes 1824768
  102.3 11.0 %copy-start.2 = (bf16[864,4096]{1,0:T(8,128)(2,1)S(1)}, bf16[864,4096]{1,0:T(8,128)(2,1)}, u32[]{:S(2)}) copy-start(bf16[864,4096]{1,0:T(8,128)(2,1)} %convert_element_type.86) | copy-start | bytes 21233668
  124.2 7.2 %copy-start.3 = (bf16[32,864]{1,0:T(8,128)(2,1)S(1)}, bf16[32,864]{1,0:T(8,128)(2,1)}, u32[]{:S(2)}) copy-start(bf16[32,864]{1,0:T(8,128)(2,1)} %param.8) | copy-start | bytes 165892
  131.3 7.4 %copy-start.4 = (f32[32,32]{1,0:T(8,128)S(1)}, f32[32,32]{1,0:T(8,128)}, u32[]{:S(2)}) copy-start(f32[32,32]{1,0:T(8,128)} %param.11) | copy-start | bytes 12292
  131.3 126.4 %all-reduce.4.cloned.1.call-start = ((), (), s32[]{:S(2)}) async-start(), calls=%async_computation.1 | async-start | bytes 229376 | tf_op jit(solution)/shard_map/psum | solution.py:79
Sparse Core Ops, SparseCore 0:
  49.9 60.6 all-gather.2
  131.5 90.0 reduce-scatter.3
  224.5 33.1 all-reduce.3
